TPU v7x, 32 devices: a whole 2x2x4 slice. The times are simulated.
32 devices in a mesh: pole: 2 (over x), row: 8 (over z, y), col: 2 (over core).
Axes of the slice: x: 2, y: 2, z: 4, core: 2. Of those that a mesh axis runs over, the one named last changes fastest.
Arguments:
- anc_inverse: bfloat16 [2048, 1024], P(('pole', 'row')), parts along dimension 0, as said below
- parent_pivinv: float32 [2048, 1024], P(('pole', 'row')), parts along dimension 0, as said below
- parent_lower: bfloat16 [2048, 1024], P(('pole', 'row')), parts along dimension 0, may hold values from -0.1875 to 0.1875
- parent_mask: int32 [4], replicated, may hold values 0 or 1
- leaf_lower_par: bfloat16 [2048, 1024], P(('pole', 'row')), parts along dimension 0, may hold values from -0.125 to 0.125
- leaf_lower_anc: bfloat16 [2048, 1024], P(('pole', 'row')), parts along dimension 0, may hold values from -0.125 to 0.125
- leaf_mask: int32 [8], replicated, may hold values 0 or 1
- leaf_pivots: float32 [2048], P(('pole', 'col')), parts along dimension 0, may hold values from 0.5 to 2
Outputs:
- parent_block: float32 [2048, 1024], P(('pole', 'row')), parts along dimension 0
- parent_offdiag: bfloat16 [2048, 1024], P(('pole', 'row'), 'col'), parts along dimension 0
- leaf_par_block: bfloat16 [2048, 1024], P(('pole', 'row'), 'col'), parts along dimension 0
- leaf_anc_block: bfloat16 [2048, 1024], P(('pole', 'row'), 'col'), parts along dimension 0
- density: float32 [2048], P(('pole', 'col')), parts along dimension 0
There are 2 independent parts, one for each index of `pole`. A program takes and returns all parts, laid end to end along the dimension named above; an argument that names none is the same for every part. Nothing has to cross between parts.
Inputs may be any that keep to these rules, and one draw needn't show every extreme that they name: `anc_inverse`: symmetric. `parent_pivinv`: symmetric. `parent_mask`: 1 marks a structurally nonzero block of 256 rows. `leaf_mask`: 1 marks a structurally nonzero block of 256 rows.
All inputs are finite; a program needn't handle non-finite values.
Results may differ from a plain program's by a relative error of at most 0.0095.
Values may be sent and summed in bfloat16 or wider, within the bound.
No kernel may reach another device: no remote copies, remote signals or barrier semaphores. Data moves between devices by JAX's collectives and lax.ppermute only.
A program may use at most 64 MiB of HBM per device.

v0:
```python
import jax
import jax.numpy as jnp
from jax import lax
from jax.sharding import PartitionSpec as P

BLOCK = 256
ORDER = 1024


def local(
    anc_inverse,
    parent_pivinv,
    parent_lower,
    parent_mask,
    leaf_lower_par,
    leaf_lower_anc,
    leaf_mask,
    leaf_pivots,
):
    row_index = lax.axis_index("row")
    row_devices = lax.axis_size("row")
    col_index = lax.axis_index("col")
    anc_rows = anc_inverse.shape[0]
    order_rows = parent_pivinv.shape[0]
    col_width = leaf_pivots.shape[0]
    parent_gate = lax.dynamic_slice_in_dim(
        jnp.repeat(parent_mask, BLOCK), row_index * anc_rows, anc_rows
    )
    lower_one = parent_lower * parent_gate[:, None].astype(jnp.bfloat16)
    lower_half = lax.dynamic_slice_in_dim(lower_one, col_index * col_width, col_width, 1)
    leaf_gate = jnp.repeat(leaf_mask, BLOCK)
    gate_par = lax.dynamic_slice_in_dim(leaf_gate[:ORDER], row_index * order_rows, order_rows)
    gate_anc = lax.dynamic_slice_in_dim(leaf_gate[ORDER:], row_index * anc_rows, anc_rows)
    leaf_local = jnp.concatenate(
        [
            leaf_lower_par * gate_par[:, None].astype(jnp.bfloat16),
            leaf_lower_anc * gate_anc[:, None].astype(jnp.bfloat16),
        ],
        axis=0,
    )
    leaf_half = lax.dynamic_slice_in_dim(leaf_local, col_index * col_width, col_width, 1)
    columns = anc_inverse
    product = jnp.dot(
        columns,
        lax.all_gather(lower_half, "row", axis=0, tiled=True),
        preferred_element_type=jnp.float32,
    )
    parent_offdiag = (-product).astype(jnp.bfloat16)
    offdiag_rows = lax.all_gather(parent_offdiag, "col", axis=1, tiled=True)
    columns = lower_one
    diag_sums = lax.psum_scatter(
        lax.dot_general(
            columns, offdiag_rows, (((0,), (0,)), ((), ())), preferred_element_type=jnp.float32
        ),
        "row",
        scatter_dimension=0,
        tiled=True,
    )
    parent_block = parent_pivinv - diag_sums
    parent_round = parent_block.astype(jnp.bfloat16)
    mirrored = lax.all_to_all(offdiag_rows, "row", split_axis=1, concat_axis=0, tiled=True).T
    upper_rows = jnp.concatenate(
        [
            parent_round.reshape(order_rows, row_devices, order_rows),
            mirrored.reshape(order_rows, row_devices, anc_rows),
        ],
        axis=2,
    )
    lower_rows = jnp.concatenate(
        [
            offdiag_rows.reshape(anc_rows, row_devices, order_rows),
            anc_inverse.reshape(anc_rows, row_devices, anc_rows),
        ],
        axis=2,
    )
    inverse_rows = jnp.concatenate(
        [upper_rows.reshape(order_rows, -1), lower_rows.reshape(anc_rows, -1)], axis=0
    )
    columns = inverse_rows
    leaf_product = jnp.dot(
        columns,
        lax.all_gather(leaf_half, "row", axis=0, tiled=True),
        preferred_element_type=jnp.float32,
    )
    leaf_result = (-leaf_product).astype(jnp.bfloat16)
    partial_sums = jnp.sum(leaf_half.astype(jnp.float32) * leaf_result.astype(jnp.float32), axis=0)
    density = leaf_pivots - lax.psum(partial_sums, "row")
    return (
        parent_block,
        parent_offdiag,
        leaf_result[:order_rows],
        leaf_result[order_rows:],
        density,
    )


def local_whole(
    anc_inverse,
    parent_pivinv,
    parent_lower,
    parent_mask,
    leaf_lower_par,
    leaf_lower_anc,
    leaf_mask,
    leaf_pivots,
):
    row_index = lax.axis_index("row")
    row_devices = lax.axis_size("row")
    col_index = lax.axis_index("col")
    anc_rows = anc_inverse.shape[0]
    order_rows = parent_pivinv.shape[0]
    col_width = leaf_pivots.shape[0]
    off_width = parent_lower.shape[1] // 2
    half = anc_rows // 2

    def mine(x):
        return lax.dynamic_slice_in_dim(x, col_index * half, half, 0)

    order_all = order_rows * row_devices
    parent_gate = jnp.repeat(parent_mask, BLOCK).astype(jnp.bfloat16)
    leaf_gate = jnp.repeat(leaf_mask, BLOCK).astype(jnp.bfloat16)
    anc_start = row_index * anc_rows + col_index * half
    order_start = row_index * order_rows + col_index * half
    lower_gate = lax.dynamic_slice_in_dim(parent_gate, anc_start, half)
    par_gate = lax.dynamic_slice_in_dim(leaf_gate[:order_all], order_start, half)
    anc_gate = lax.dynamic_slice_in_dim(leaf_gate[order_all:], anc_start, half)
    stacked = jnp.stack(
        [
            mine(anc_inverse),
            mine(parent_lower) * lower_gate[:, None],
            mine(leaf_lower_par) * par_gate[:, None],
            mine(leaf_lower_anc) * anc_gate[:, None],
        ]
    )
    full = lax.all_gather(stacked, ("row", "col"), axis=1, tiled=True)
    anc_full, lower_m, par_m, anc_m = (full[0], full[1], full[2], full[3])
    offdiag_all = (-jnp.dot(anc_full, lower_m, preferred_element_type=jnp.float32)).astype(
        jnp.bfloat16
    )
    lower_cols = lax.dynamic_slice_in_dim(lower_m, row_index * order_rows, order_rows, 1)
    parent_block = parent_pivinv - lax.dot_general(
        lower_cols, offdiag_all, (((0,), (0,)), ((), ())), preferred_element_type=jnp.float32
    )
    parent_round = parent_block.astype(jnp.bfloat16)
    par_half = lax.dynamic_slice_in_dim(par_m, col_index * col_width, col_width, 1)
    anc_half = lax.dynamic_slice_in_dim(anc_m, col_index * col_width, col_width, 1)
    offdiag_cols = lax.dynamic_slice_in_dim(offdiag_all, row_index * order_rows, order_rows, 1)
    offdiag_rows = lax.dynamic_slice_in_dim(offdiag_all, row_index * anc_rows, anc_rows, 0)
    upper_sum = jnp.dot(
        parent_round, par_half, preferred_element_type=jnp.float32
    ) + lax.dot_general(
        offdiag_cols, anc_half, (((0,), (0,)), ((), ())), preferred_element_type=jnp.float32
    )
    lower_sum = jnp.dot(offdiag_rows, par_half, preferred_element_type=jnp.float32) + jnp.dot(
        anc_inverse, anc_half, preferred_element_type=jnp.float32
    )
    leaf_par_block = (-upper_sum).astype(jnp.bfloat16)
    leaf_anc_block = (-lower_sum).astype(jnp.bfloat16)
    par_own = lax.dynamic_slice_in_dim(par_half, row_index * order_rows, order_rows, 0)
    anc_own = lax.dynamic_slice_in_dim(anc_half, row_index * anc_rows, anc_rows, 0)
    partial_sums = jnp.sum(
        par_own.astype(jnp.float32) * leaf_par_block.astype(jnp.float32), axis=0
    ) + jnp.sum(anc_own.astype(jnp.float32) * leaf_anc_block.astype(jnp.float32), axis=0)
    spread = jnp.broadcast_to(partial_sums[None], (row_devices, col_width))
    column_sums = jnp.sum(lax.all_to_all(spread, "row", 0, 0, tiled=True), axis=0)
    density = leaf_pivots - column_sums
    offdiag_own = lax.dynamic_slice_in_dim(offdiag_rows, col_index * off_width, off_width, 1)
    return (parent_block, offdiag_own, leaf_par_block, leaf_anc_block, density)


def fits_whole(mesh, anc_rows, order_rows, order_cols, leaf_cols):
    anc_all = anc_rows * mesh.shape["row"]
    return (
        anc_rows == order_rows
        and anc_rows % 2 == 0
        and (len({anc_all, order_cols, leaf_cols}) == 1)
        and (anc_all * anc_all * 2 <= 16 * 1024 * 1024)
    )


def solution(mesh):
    placed = (
        P(("pole", "row"), None),
        P(("pole", "row"), None),
        P(("pole", "row"), None),
        P(),
        P(("pole", "row"), None),
        P(("pole", "row"), None),
        P(),
        P(("pole", "col")),
    )
    placed_out = (
        P(("pole", "row"), None),
        P(("pole", "row"), "col"),
        P(("pole", "row"), "col"),
        P(("pole", "row"), "col"),
        P(("pole", "col")),
    )
    shards = mesh.shape["pole"] * mesh.shape["row"]

    def run(*args):
        anc_rows = args[0].shape[0] // shards
        order_rows = args[1].shape[0] // shards
        body = (
            local_whole
            if fits_whole(mesh, anc_rows, order_rows, args[2].shape[1], args[4].shape[1])
            else local
        )
        return jax.shard_map(
            body, mesh=mesh, in_specs=placed, out_specs=placed_out, check_vma=False
        )(*args)

    return run
```

profile of v0, /device:TPU:0, one launch (start us, length us, event | category | flops | bytes accessed | tf_op | source)
XLA Modules:
  0.0 118.8 jit_solution(13952267705256480365)
XLA Ops:
  7.2 0.0 all-gather.2.cloned.1.call-start
  7.2 0.7 convert_element_type.44
  7.9 0.1 fusion.30
  8.0 0.1 broadcast_bitcast_fusion.1
  8.0 0.1 broadcast_bitcast_fusion
  8.1 0.1 dynamic_slice.55
  8.2 0.1 dynamic_slice.57
  8.3 0.7 convert_element_type.42
  8.9 0.1 broadcast_bitcast_fusion.2
  9.0 0.1 dynamic_slice.53
  9.1 1.1 multiply_bitcast_fusion.2
  10.1 1.1 multiply_bitcast_fusion
  11.2 0.9 pad_maximum_fusion
  12.1 0.0 all-gather.2.cloned.1.call-update
  12.1 77.8 %all-gather.2.cloned.1.call-done = bf16[4,1024,1024]{2,1,0:T(8,128)(2,1)} async-done(((bf16[4,64,1024]{2,1,0:T(8,128)(2,1)}), bf16[4,1024,1024]{2,1,0:T(8,128)(2,1)}) %all-gather.2.cloned.1.call-update) | async-done | bytes 8388624 | tf_op jit(solution)/shard_map/all_gather | solution.py:135
  89.9 0.0 copy-start
  89.9 3.8 %fusion.29 = (bf16[1,1024,1024]{2,1,0:T(8,128)(2,1)S(1)}, bf16[1,1024,1024]{2,1,0:T(8,128)(2,1)S(1)}, bf16[1,1024,1024]{2,1,0:T(8,128)(2,1)S(1)}) fusion(bf16[4,1024,1024]{2,1,0:T(8,128)(2,1)} %all-gather.2.cloned.1.call-done), kind=kLoop, calls=%fused_computation.44 | loop fusion | bytes 12582912 | tf_op jit(solution)/shard_map/slice | solution.py:136
  93.7 1.5 %copy-done = bf16[4,1024,1024]{2,1,0:T(8,128)(2,1)S(1)} copy-done((bf16[4,1024,1024]{2,1,0:T(8,128)(2,1)S(1)}, bf16[4,1024,1024]{2,1,0:T(8,128)(2,1)}, u32[]{:S(2)}) %copy-start) | copy-done | bytes 8388632
  95.1 0.0 copy-start.3
  95.2 2.3 %negate_convert_fusion = bf16[1024,1024]{1,0:T(8,128)(2,1)S(1)} fusion(bf16[4,1024,1024]{2,1,0:T(8,128)(2,1)S(1)} %copy-done), kind=kOutput, calls=%fused_computation | convolution fusion | flops 2149580800 | bytes 6291456 | tf_op jit(solution)/shard_map/dot_general | solution.py:137
  97.5 0.3 fusion.8
  97.8 0.0 copy-done.3
  97.8 0.0 copy-start.2
  97.8 0.5 convolution_subtract_fusion
  98.3 0.0 copy-start.1
  98.3 0.3 fusion.10
  98.7 0.0 copy-start.4
  98.7 0.1 copy-done.2
  98.8 1.0 fusion.16
  99.8 1.1 fusion.17
  100.9 0.0 copy-done.1
  100.9 0.6 broadcast_in_dim.20
  101.5 3.3 %all-to-all-start = ((f32[8,1,512]{2,1,0:T(1,128)}), f32[8,1,512]{2,1,0:T(1,128)S(1)}, u32[]{:S(2)}, u32[]{:S(2)}) async-start(f32[8,1,512]{2,1,0:T(1,128)} %broadcast_in_dim.20), calls=%async_computation | async-start | bytes 32768 | tf_op jit(solution)/shard_map/all_to_all | solution.py:165
  104.8 0.8 dynamic_slice.60
  105.6 5.7 %all-to-all-done = f32[8,1,512]{2,1,0:T(1,128)S(1)} async-done(((f32[8,1,512]{2,1,0:T(1,128)}), f32[8,1,512]{2,1,0:T(1,128)S(1)}, u32[]{:S(2)}, u32[]{:S(2)}) %all-to-all-start) | async-done | bytes 16416 | tf_op jit(solution)/shard_map/all_to_all | solution.py:165
  111.3 0.0 copy-done.4
  111.3 0.6 sub.7
  (5 shorter events, 0.1 us)
Async XLA Ops:
  7.2 82.7 %all-gather.2.cloned.1.call-start = ((), (), s32[]{:S(2)}) async-start(), calls=%async_computation.1 | async-start | bytes 8912896 | tf_op jit(solution)/shard_map/all_gather | solution.py:135
  89.9 5.2 %copy-start = (bf16[4,1024,1024]{2,1,0:T(8,128)(2,1)S(1)}, bf16[4,1024,1024]{2,1,0:T(8,128)(2,1)}, u32[]{:S(2)}) copy-start(bf16[4,1024,1024]{2,1,0:T(8,128)(2,1)} %all-gather.2.cloned.1.call-done) | copy-start | bytes 25165828
  95.1 2.7 %copy-start.3 = (f32[128,1024]{1,0:T(8,128)S(1)}, f32[128,1024]{1,0:T(8,128)}, u32[]{:S(2)}) copy-start(f32[128,1024]{1,0:T(8,128)} %param.9) | copy-start | bytes 1572868
  97.8 1.0 copy-start.2
  98.3 2.5 %copy-start.1 = (f32[128,1024]{1,0:T(8,128)}, f32[128,1024]{1,0:T(8,128)S(1)}, u32[]{:S(2)}) copy-start(f32[128,1024]{1,0:T(8,128)S(1)} %convolution_subtract_fusion) | copy-start | bytes 1572868
  98.7 12.7 %copy-start.4 = (f32[512]{0:T(512)S(1)}, f32[512]{0:T(512)}, u32[]{:S(2)}) copy-start(f32[512]{0:T(512)} %param.15) | copy-start | bytes 6148
  101.5 9.8 %all-to-all-start = ((f32[8,1,512]{2,1,0:T(1,128)}), f32[8,1,512]{2,1,0:T(1,128)S(1)}, u32[]{:S(2)}, u32[]{:S(2)}) async-start(f32[8,1,512]{2,1,0:T(1,128)} %broadcast_in_dim.20), calls=%async_computation | async-start | bytes 32768 | tf_op jit(solution)/shard_map/all_to_all | solution.py:165
Sparse Core Ops, SparseCore 0:
  12.2 77.6 all-gather.1
where the time goes:
time: 119 us
  waiting for transfers between devices  83.5 us (70%)
  between operations  14.2 us (12%)
  local copies, waits for them, and re-layouts  7.3 us (6%)
  matrix products  5.52 us (5%)
  other arithmetic  4.94 us (4%)
  starting transfers between devices  3.36 us (3%)
    all_gather x1, waiting for transfers between devices, local_whole(): full = lax.all_gather(stacked, ('row', 'col'), axis=1, tiled=True)  77.8 us
    all_to_all x1, waiting for transfers between devices, local_whole(): lax.all_to_all(spread, 'row', 0, 0, tiled=True)  5.73 us
    slice x1, local copies, waits for them, and re-layouts, local_whole(): anc_full, lower_m, par_m, anc_m = (full[0], full[1], full[2], full[3])  3.75 us
    all_to_all x1, starting transfers between devices, local_whole(): lax.all_to_all(spread, 'row', 0, 0, tiled=True)  3.32 us
    another operation x3, other arithmetic, local_whole(): jnp.stack([mine(anc_inverse), mine(parent_lower) * lower_gate[:, None], m...  3 us
  transfers between devices with their start and end apart: 2, of which 2 were waited for; matrix products, arithmetic and copies ran while one was open for 1% of the time, Pallas kernels for 0%

commit v1 on v0

--- a/solution.py
+++ b/solution.py
@@ -132,7 +132,24 @@
             mine(leaf_lower_anc) * anc_gate[:, None],
         ]
     )
-    full = lax.all_gather(stacked, ("row", "col"), axis=1, tiled=True)
+    r1 = lax.axis_size(("row", "col"))
+    small, lower, last = (r1, lax.axis_index(("row", "col")), stacked.shape[1])
+    queue = tuple(((q, (q + 1) % small) for q in range(small)))
+    by_place = tuple(((q, (q - 1) % small) for q in range(small)))
+    full = jnp.zeros((*stacked.shape[:1], small * last, *stacked.shape[2:]), stacked.dtype)
+    full = lax.dynamic_update_slice_in_dim(full, stacked, lower * last, axis=1)
+    tmp = value_now = stacked
+    work_now = small // 2
+    jj = 1
+    while jj < work_now + 1:
+        tmp = lax.ppermute(tmp, ("row", "col"), queue)
+        full = lax.dynamic_update_slice_in_dim(full, tmp, (lower - jj) % small * last, axis=1)
+        if jj < small - work_now:
+            value_now = lax.ppermute(value_now, ("row", "col"), by_place)
+            full = lax.dynamic_update_slice_in_dim(
+                full, value_now, (lower + jj) % small * last, axis=1
+            )
+        jj = jj + 1
     anc_full, lower_m, par_m, anc_m = (full[0], full[1], full[2], full[3])
     offdiag_all = (-jnp.dot(anc_full, lower_m, preferred_element_type=jnp.float32)).astype(
         jnp.bfloat16

time: 119 us -> 143 us (1.20)
  starting transfers between devices: 3.36 us -> 68 us
  waiting for transfers between devices: 83.5 us -> 33.5 us
  local copies, waits for them, and re-layouts: 7.3 us -> 27.4 us
  between operations: 14.2 us -> 0.79 us
  matrix products: 5.52 us -> 7.82 us
    all_gather x1 -> x0, waiting for transfers between devices: 77.8 us -> none  [local_whole(): full = lax.all_gather(stacked, ('row', 'col'), axis=1, tiled=True)]
    ppermute x0 -> x15, starting transfers between devices: none -> 60.1 us  [the longest x8 52.9 us: local_whole(): tmp = lax.ppermute(tmp, ('row', 'col'), queue)]
    ppermute x0 -> x15, waiting for transfers between devices: none -> 27.7 us  [the longest x8 27.7 us: local_whole(): tmp = lax.ppermute(tmp, ('row', 'col'), queue)]
    dynamic_update_slice x0 -> x15, local copies, waits for them, and re-layouts: none -> 17.5 us  [the longest x8 10.8 us: local_whole(): lax.dynamic_update_slice_in_dim(full, tmp, (lower - jj) % small * last, a...]
    all_to_all x1, starting transfers between devices: 3.32 us -> 7.98 us  [local_whole(): lax.all_to_all(spread, 'row', 0, 0, tiled=True)]
    broadcast_in_dim x0 -> x1, local copies, waits for them, and re-layouts: none -> 4.32 us  [local_whole(): jnp.zeros((*stacked.shape[:1], small * last, *stacked.shape[2:]), stacked...]
    dot_general x1, matrix products: 2.33 us -> 4.62 us  [local_whole(): jnp.dot(anc_full, lower_m, preferred_element_type=jnp.float32)]
    unnamed x16 -> x18, local copies, waits for them, and re-layouts: 1.85 us -> 0.27 us
  transfers between devices with their start and end apart: 2 -> 16, of which waited for: 2 -> 6; matrix products, arithmetic and copies ran while one was open for 1% -> 12% of each run, Pallas kernels for 0% -> 0%
where the time goes in v1:
time: 143 us
  starting transfers between devices  68 us (48%)
  waiting for transfers between devices  33.5 us (23%)
  local copies, waits for them, and re-layouts  27.4 us (19%)
  matrix products  7.82 us (5%)
  other arithmetic  4.97 us (3%)
    ppermute x8, starting transfers between devices, local_whole(): tmp = lax.ppermute(tmp, ('row', 'col'), queue)  52.9 us
    ppermute x8, waiting for transfers between devices, local_whole(): tmp = lax.ppermute(tmp, ('row', 'col'), queue)  27.7 us
    dynamic_update_slice x8, local copies, waits for them, and re-layouts, local_whole(): lax.dynamic_update_slice_in_dim(full, tmp, (lower - jj) % small * last, a...  10.8 us
    all_to_all x1, starting transfers between devices, local_whole(): lax.all_to_all(spread, 'row', 0, 0, tiled=True)  7.98 us
    ppermute x7, starting transfers between devices, local_whole(): value_now = lax.ppermute(value_now, ('row', 'col'), by_place)  7.17 us
    dynamic_update_slice x7, local copies, waits for them, and re-layouts, local_whole(): lax.dynamic_update_slice_in_dim(full, value_now, (lower + jj) % small * l...  6.78 us
    all_to_all x1, waiting for transfers between devices, local_whole(): lax.all_to_all(spread, 'row', 0, 0, tiled=True)  5.8 us
    dot_general x1, matrix products, local_whole(): jnp.dot(anc_full, lower_m, preferred_element_type=jnp.float32)  4.62 us
  transfers between devices with their start and end apart: 16, of which 6 were waited for; matrix products, arithmetic and copies ran while one was open for 12% of the time, Pallas kernels for 0%

profile of v1, /device:TPU:0, one launch (start us, length us, event | category | flops | bytes accessed | tf_op | source)
XLA Modules:
  0.0 142.6 jit_solution(5554757479583187245)
XLA Ops:
  0.6 0.7 convert_element_type.44
  1.7 0.7 convert_element_type.42
  2.5 1.1 multiply_bitcast_fusion.2
  3.6 1.1 multiply_bitcast_fusion
  4.7 4.3 %broadcast_in_dim.20 = bf16[4,1024,1024]{2,1,0:T(8,128)(2,1)} broadcast(bf16[]{:T(256)} %constant.140.clone.1), dimensions={} | broadcast | bytes 8388610 | tf_op jit(solution)/shard_map/broadcast_in_dim | solution.py:139
  9.0 0.9 pad_maximum_fusion
  9.9 0.5 collective-permute-start
  10.3 5.0 %collective-permute-start.1 = (bf16[4,64,1024]{2,1,0:T(8,128)(2,1)S(1)}, bf16[4,64,1024]{2,1,0:T(8,128)(2,1)S(1)}, u32[]{:S(2)}, u32[]{:S(2)}) collective-permute-start(bf16[4,64,1024]{2,1,0:T(8,128)(2,1)S(1)} %get-tuple-element.8), channel_id=1, source_target_pairs={{0,15},{1,0},{2,1},{3,2},{4,3},{5,4},{6,5},{7,6},{8,7},{9,8},{10,9... | collective-permute-start | bytes 1572872 | tf_op jit(solution)/shard_map/ppermute | solution.py:148
  15.4 7.0 %collective-permute-done = bf16[4,64,1024]{2,1,0:T(8,128)(2,1)S(1)} collective-permute-done((bf16[4,64,1024]{2,1,0:T(8,128)(2,1)S(1)}, bf16[4,64,1024]{2,1,0:T(8,128)(2,1)S(1)}, u32[]{:S(2)}, u32[]{:S(2)}) %collective-permute-start) | collective-permute-done | bytes 524320 | tf_op jit(solution)/shard_map/ppermute | solution.py:145
  22.3 2.4 %collective-permute-start.2 = (bf16[4,64,1024]{2,1,0:T(8,128)(2,1)S(1)}, bf16[4,64,1024]{2,1,0:T(8,128)(2,1)S(1)}, u32[]{:S(2)}, u32[]{:S(2)}) collective-permute-start(bf16[4,64,1024]{2,1,0:T(8,128)(2,1)S(1)} %collective-permute-done), channel_id=1, source_target_pairs={{0,1},{1,2},{2,3},{3,4},{4,5},{5,6},{6,7},{7,8},{8,9},{9,10},{10,1... | collective-permute-start | bytes 1572872 | tf_op jit(solution)/shard_map/ppermute | solution.py:145
  24.7 2.0 %collective-permute-start.3 = (bf16[4,64,1024]{2,1,0:T(8,128)(2,1)S(1)}, bf16[4,64,1024]{2,1,0:T(8,128)(2,1)S(1)}, u32[]{:S(2)}, u32[]{:S(2)}) collective-permute-start(bf16[4,64,1024]{2,1,0:T(8,128)(2,1)S(1)} %collective-permute-done.1), channel_id=1, source_target_pairs={{0,15},{1,0},{2,1},{3,2},{4,3},{5,4},{6,5},{7,6},{8,7},{9,8},{10,9... | collective-permute-start | bytes 1572872 | tf_op jit(solution)/shard_map/ppermute | solution.py:148
  26.8 7.0 %collective-permute-done.2 = bf16[4,64,1024]{2,1,0:T(8,128)(2,1)S(1)} collective-permute-done((bf16[4,64,1024]{2,1,0:T(8,128)(2,1)S(1)}, bf16[4,64,1024]{2,1,0:T(8,128)(2,1)S(1)}, u32[]{:S(2)}, u32[]{:S(2)}) %collective-permute-start.2) | collective-permute-done | bytes 524320 | tf_op jit(solution)/shard_map/ppermute | solution.py:145
  33.8 4.4 %collective-permute-start.4 = (bf16[4,64,1024]{2,1,0:T(8,128)(2,1)S(1)}, bf16[4,64,1024]{2,1,0:T(8,128)(2,1)S(1)}, u32[]{:S(2)}, u32[]{:S(2)}) collective-permute-start(bf16[4,64,1024]{2,1,0:T(8,128)(2,1)S(1)} %collective-permute-done.2), channel_id=1, source_target_pairs={{0,1},{1,2},{2,3},{3,4},{4,5},{5,6},{6,7},{7,8},{8,9},{9,10},{10,1... | collective-permute-start | bytes 1572872 | tf_op jit(solution)/shard_map/ppermute | solution.py:145
  38.2 7.0 %collective-permute-done.4 = bf16[4,64,1024]{2,1,0:T(8,128)(2,1)S(1)} collective-permute-done((bf16[4,64,1024]{2,1,0:T(8,128)(2,1)S(1)}, bf16[4,64,1024]{2,1,0:T(8,128)(2,1)S(1)}, u32[]{:S(2)}, u32[]{:S(2)}) %collective-permute-start.4) | collective-permute-done | bytes 524320 | tf_op jit(solution)/shard_map/ppermute | solution.py:145
  45.2 6.5 %collective-permute-start.6 = (bf16[4,64,1024]{2,1,0:T(8,128)(2,1)S(1)}, bf16[4,64,1024]{2,1,0:T(8,128)(2,1)S(1)}, u32[]{:S(2)}, u32[]{:S(2)}) collective-permute-start(bf16[4,64,1024]{2,1,0:T(8,128)(2,1)S(1)} %collective-permute-done.4), channel_id=1, source_target_pairs={{0,1},{1,2},{2,3},{3,4},{4,5},{5,6},{6,7},{7,8},{8,9},{9,10},{10,1... | collective-permute-start | bytes 1572872 | tf_op jit(solution)/shard_map/ppermute | solution.py:145
  51.7 4.8 %collective-permute-done.6 = bf16[4,64,1024]{2,1,0:T(8,128)(2,1)S(1)} collective-permute-done((bf16[4,64,1024]{2,1,0:T(8,128)(2,1)S(1)}, bf16[4,64,1024]{2,1,0:T(8,128)(2,1)S(1)}, u32[]{:S(2)}, u32[]{:S(2)}) %collective-permute-start.6) | collective-permute-done | bytes 524320 | tf_op jit(solution)/shard_map/ppermute | solution.py:145
  56.5 9.4 %collective-permute-start.8 = (bf16[4,64,1024]{2,1,0:T(8,128)(2,1)S(1)}, bf16[4,64,1024]{2,1,0:T(8,128)(2,1)}, u32[]{:S(2)}, u32[]{:S(2)}) collective-permute-start(bf16[4,64,1024]{2,1,0:T(8,128)(2,1)S(1)} %collective-permute-done.6), channel_id=1, source_target_pairs={{0,1},{1,2},{2,3},{3,4},{4,5},{5,6},{6,7},{7,8},{8,9},{9,10},{10,1... | collective-permute-start | bytes 1572872 | tf_op jit(solution)/shard_map/ppermute | solution.py:145
  66.0 2.0 %collective-permute-done.8 = bf16[4,64,1024]{2,1,0:T(8,128)(2,1)} collective-permute-done((bf16[4,64,1024]{2,1,0:T(8,128)(2,1)S(1)}, bf16[4,64,1024]{2,1,0:T(8,128)(2,1)}, u32[]{:S(2)}, u32[]{:S(2)}) %collective-permute-start.8) | collective-permute-done | bytes 524320 | tf_op jit(solution)/shard_map/ppermute | solution.py:145
  68.0 12.1 %collective-permute-start.10 = (bf16[4,64,1024]{2,1,0:T(8,128)(2,1)}, bf16[4,64,1024]{2,1,0:T(8,128)(2,1)}, u32[]{:S(2)}, u32[]{:S(2)}) collective-permute-start(bf16[4,64,1024]{2,1,0:T(8,128)(2,1)} %collective-permute-done.8), channel_id=1, source_target_pairs={{0,1},{1,2},{2,3},{3,4},{4,5},{5,6},{6,7},{7,8},{8,9},{9,10},{10,1... | collective-permute-start | bytes 1572872 | tf_op jit(solution)/shard_map/ppermute | solution.py:145
  80.1 0.8 constant_dynamic-update-slice_fusion.14
  81.0 0.8 constant_dynamic-update-slice_fusion.13
  81.8 1.9 %constant_dynamic-update-slice_fusion.12 = bf16[4,1024,1024]{2,1,0:T(8,128)(2,1)} fusion(bf16[4,1024,1024]{2,1,0:T(8,128)(2,1)} %constant_dynamic-update-slice_fusion.13, bf16[4,64,1024]{2,1,0:T(8,128)(2,1)} %copy-done.3, s32[]{:T(128)S(6)} %select_n.146), kind=kLoop, calls=%fused_computation.51 | loop fusion | bytes 1048580 | tf_op jit(solution)/shard_map/dynamic_update_slice | solution.py:146
  83.6 0.8 constant_dynamic-update-slice_fusion.11
  84.5 10.3 %collective-permute-start.12 = (bf16[4,64,1024]{2,1,0:T(8,128)(2,1)}, bf16[4,64,1024]{2,1,0:T(8,128)(2,1)S(1)}, u32[]{:S(2)}, u32[]{:S(2)}) collective-permute-start(bf16[4,64,1024]{2,1,0:T(8,128)(2,1)} %collective-permute-done.10), channel_id=1, source_target_pairs={{0,1},{1,2},{2,3},{3,4},{4,5},{5,6},{6,7},{7,8},{8,9},{9,10},{10,1... | collective-permute-start | bytes 1572872 | tf_op jit(solution)/shard_map/ppermute | solution.py:145
  94.7 0.8 constant_dynamic-update-slice_fusion.10
  95.6 0.8 constant_dynamic-update-slice_fusion.9
  96.4 1.9 %constant_dynamic-update-slice_fusion.8 = bf16[4,1024,1024]{2,1,0:T(8,128)(2,1)} fusion(bf16[4,1024,1024]{2,1,0:T(8,128)(2,1)} %constant_dynamic-update-slice_fusion.9, bf16[4,64,1024]{2,1,0:T(8,128)(2,1)} %copy-done.2, s32[]{:T(128)S(6)} %select_n.154), kind=kLoop, calls=%fused_computation.47 | loop fusion | bytes 1048580 | tf_op jit(solution)/shard_map/dynamic_update_slice | solution.py:146
  98.3 1.9 %constant_dynamic-update-slice_fusion.7 = bf16[4,1024,1024]{2,1,0:T(8,128)(2,1)} fusion(bf16[4,1024,1024]{2,1,0:T(8,128)(2,1)} %constant_dynamic-update-slice_fusion.8, bf16[4,64,1024]{2,1,0:T(8,128)(2,1)} %collective-permute-done.7, s32[]{:T(128)S(6)} %select_n.156), kind=kLoop, calls=%fused_computation.46 | loop fusion | bytes 1048580 | tf_op jit(solution)/shard_map/dynamic_update_slice | solution.py:149
  100.1 1.9 %constant_dynamic-update-slice_fusion.6 = bf16[4,1024,1024]{2,1,0:T(8,128)(2,1)} fusion(bf16[4,1024,1024]{2,1,0:T(8,128)(2,1)} %constant_dynamic-update-slice_fusion.7, bf16[4,64,1024]{2,1,0:T(8,128)(2,1)} %collective-permute-done.8, s32[]{:T(128)S(6)} %select_n.158), kind=kLoop, calls=%fused_computation.45 | loop fusion | bytes 1048580 | tf_op jit(solution)/shard_map/dynamic_update_slice | solution.py:146
  102.0 7.3 %collective-permute-start.14 = (bf16[4,64,1024]{2,1,0:T(8,128)(2,1)S(1)}, bf16[4,64,1024]{2,1,0:T(8,128)(2,1)S(1)}, u32[]{:S(2)}, u32[]{:S(2)}) collective-permute-start(bf16[4,64,1024]{2,1,0:T(8,128)(2,1)S(1)} %collective-permute-done.12), channel_id=1, source_target_pairs={{0,1},{1,2},{2,3},{3,4},{4,5},{5,6},{6,7},{7,8},{8,9},{9,10},{10,1... | collective-permute-start | bytes 1572872 | tf_op jit(solution)/shard_map/ppermute | solution.py:145
  109.3 0.8 constant_dynamic-update-slice_fusion.5
  110.1 1.9 %constant_dynamic-update-slice_fusion.4 = bf16[4,1024,1024]{2,1,0:T(8,128)(2,1)} fusion(bf16[4,1024,1024]{2,1,0:T(8,128)(2,1)} %constant_dynamic-update-slice_fusion.5, bf16[4,64,1024]{2,1,0:T(8,128)(2,1)} %collective-permute-done.10, s32[]{:T(128)S(6)} %select_n.162), kind=kLoop, calls=%fused_computation.43 | loop fusion | bytes 1048580 | tf_op jit(solution)/shard_map/dynamic_update_slice | solution.py:146
  112.0 0.8 constant_dynamic-update-slice_fusion.3
  112.8 0.8 constant_dynamic-update-slice_fusion.2
  113.6 0.8 constant_dynamic-update-slice_fusion.1
  114.4 0.8 constant_dynamic-update-slice_fusion
  115.3 3.6 %fusion.27 = (bf16[1,1024,1024]{2,1,0:T(8,128)(2,1)S(1)}, bf16[1,1024,1024]{2,1,0:T(8,128)(2,1)S(1)}, bf16[1,1024,1024]{2,1,0:T(8,128)(2,1)S(1)}) fusion(bf16[4,1024,1024]{2,1,0:T(8,128)(2,1)} %constant_dynamic-update-slice_fusion), kind=kLoop, calls=%fused_computation.59 | loop fusion | bytes 12582912 | tf_op jit(solution)/shard_map/slice | solution.py:153
  118.9 4.6 %negate_convert_fusion = bf16[1024,1024]{1,0:T(8,128)(2,1)S(1)} fusion(bf16[4,1024,1024]{2,1,0:T(8,128)(2,1)} %constant_dynamic-update-slice_fusion), kind=kOutput, calls=%fused_computation | convolution fusion | flops 2149580800 | bytes 6291456 | tf_op jit(solution)/shard_map/dot_general | solution.py:154
  123.5 0.3 convolution_bitcast_fusion
  123.8 0.3 fusion.6
  124.2 0.5 convolution_subtract_fusion
  124.7 1.0 fusion.14
  125.7 1.0 fusion.15
  126.8 0.6 broadcast_in_dim.24
  127.4 8.0 %all-to-all-start = ((f32[8,1,512]{2,1,0:T(1,128)}), f32[8,1,512]{2,1,0:T(1,128)S(1)}, u32[]{:S(2)}, u32[]{:S(2)}) async-start(f32[8,1,512]{2,1,0:T(1,128)} %broadcast_in_dim.24), calls=%async_computation | async-start | bytes 32768 | tf_op jit(solution)/shard_map/all_to_all | solution.py:182
  135.4 0.8 dynamic_slice.60
  136.1 5.8 %all-to-all-done = f32[8,1,512]{2,1,0:T(1,128)S(1)} async-done(((f32[8,1,512]{2,1,0:T(1,128)}), f32[8,1,512]{2,1,0:T(1,128)S(1)}, u32[]{:S(2)}, u32[]{:S(2)}) %all-to-all-start) | async-done | bytes 16416 | tf_op jit(solution)/shard_map/all_to_all | solution.py:182
  142.0 0.6 sub.39
  (39 shorter events, 0.7 us)
Async XLA Ops:
  9.9 12.5 %collective-permute-start = (bf16[4,64,1024]{2,1,0:T(8,128)(2,1)S(1)}, bf16[4,64,1024]{2,1,0:T(8,128)(2,1)S(1)}, u32[]{:S(2)}, u32[]{:S(2)}) collective-permute-start(bf16[4,64,1024]{2,1,0:T(8,128)(2,1)S(1)} %get-tuple-element.8), channel_id=1, source_target_pairs={{0,1},{1,2},{2,3},{3,4},{4,5},{5,6},{6,7},{7,8},{8,9},{9,10},{10,1... | collective-permute-start | bytes 1572872 | tf_op jit(solution)/shard_map/ppermute | solution.py:145
  10.3 14.4 %collective-permute-start.1 = (bf16[4,64,1024]{2,1,0:T(8,128)(2,1)S(1)}, bf16[4,64,1024]{2,1,0:T(8,128)(2,1)S(1)}, u32[]{:S(2)}, u32[]{:S(2)}) collective-permute-start(bf16[4,64,1024]{2,1,0:T(8,128)(2,1)S(1)} %get-tuple-element.8), channel_id=1, source_target_pairs={{0,15},{1,0},{2,1},{3,2},{4,3},{5,4},{6,5},{7,6},{8,7},{9,8},{10,9... | collective-permute-start | bytes 1572872 | tf_op jit(solution)/shard_map/ppermute | solution.py:148
  22.3 11.4 %collective-permute-start.2 = (bf16[4,64,1024]{2,1,0:T(8,128)(2,1)S(1)}, bf16[4,64,1024]{2,1,0:T(8,128)(2,1)S(1)}, u32[]{:S(2)}, u32[]{:S(2)}) collective-permute-start(bf16[4,64,1024]{2,1,0:T(8,128)(2,1)S(1)} %collective-permute-done), channel_id=1, source_target_pairs={{0,1},{1,2},{2,3},{3,4},{4,5},{5,6},{6,7},{7,8},{8,9},{9,10},{10,1... | collective-permute-start | bytes 1572872 | tf_op jit(solution)/shard_map/ppermute | solution.py:145
  24.7 13.4 %collective-permute-start.3 = (bf16[4,64,1024]{2,1,0:T(8,128)(2,1)S(1)}, bf16[4,64,1024]{2,1,0:T(8,128)(2,1)S(1)}, u32[]{:S(2)}, u32[]{:S(2)}) collective-permute-start(bf16[4,64,1024]{2,1,0:T(8,128)(2,1)S(1)} %collective-permute-done.1), channel_id=1, source_target_pairs={{0,15},{1,0},{2,1},{3,2},{4,3},{5,4},{6,5},{7,6},{8,7},{9,8},{10,9... | collective-permute-start | bytes 1572872 | tf_op jit(solution)/shard_map/ppermute | solution.py:148
  33.7 32.1 %copy-start.3 = (bf16[4,64,1024]{2,1,0:T(8,128)(2,1)}, bf16[4,64,1024]{2,1,0:T(8,128)(2,1)S(1)}, u32[]{:S(2)}) copy-start(bf16[4,64,1024]{2,1,0:T(8,128)(2,1)S(1)} %collective-permute-done.2) | copy-start | bytes 1572868
  33.8 11.4 %collective-permute-start.4 = (bf16[4,64,1024]{2,1,0:T(8,128)(2,1)S(1)}, bf16[4,64,1024]{2,1,0:T(8,128)(2,1)S(1)}, u32[]{:S(2)}, u32[]{:S(2)}) collective-permute-start(bf16[4,64,1024]{2,1,0:T(8,128)(2,1)S(1)} %collective-permute-done.2), channel_id=1, source_target_pairs={{0,1},{1,2},{2,3},{3,4},{4,5},{5,6},{6,7},{7,8},{8,9},{9,10},{10,1... | collective-permute-start | bytes 1572872 | tf_op jit(solution)/shard_map/ppermute | solution.py:145
  38.2 13.5 %collective-permute-start.5 = (bf16[4,64,1024]{2,1,0:T(8,128)(2,1)S(1)}, bf16[4,64,1024]{2,1,0:T(8,128)(2,1)S(1)}, u32[]{:S(2)}, u32[]{:S(2)}) collective-permute-start(bf16[4,64,1024]{2,1,0:T(8,128)(2,1)S(1)} %collective-permute-done.3), channel_id=1, source_target_pairs={{0,15},{1,0},{2,1},{3,2},{4,3},{5,4},{6,5},{7,6},{8,7},{9,8},{10,9... | collective-permute-start | bytes 1572872 | tf_op jit(solution)/shard_map/ppermute | solution.py:148
  45.2 11.3 %collective-permute-start.6 = (bf16[4,64,1024]{2,1,0:T(8,128)(2,1)S(1)}, bf16[4,64,1024]{2,1,0:T(8,128)(2,1)S(1)}, u32[]{:S(2)}, u32[]{:S(2)}) collective-permute-start(bf16[4,64,1024]{2,1,0:T(8,128)(2,1)S(1)} %collective-permute-done.4), channel_id=1, source_target_pairs={{0,1},{1,2},{2,3},{3,4},{4,5},{5,6},{6,7},{7,8},{8,9},{9,10},{10,1... | collective-permute-start | bytes 1572872 | tf_op jit(solution)/shard_map/ppermute | solution.py:145
  51.7 14.2 %collective-permute-start.7 = (bf16[4,64,1024]{2,1,0:T(8,128)(2,1)S(1)}, bf16[4,64,1024]{2,1,0:T(8,128)(2,1)}, u32[]{:S(2)}, u32[]{:S(2)}) collective-permute-start(bf16[4,64,1024]{2,1,0:T(8,128)(2,1)S(1)} %collective-permute-done.5), channel_id=1, source_target_pairs={{0,15},{1,0},{2,1},{3,2},{4,3},{5,4},{6,5},{7,6},{8,7},{9,8},{10,9... | collective-permute-start | bytes 1572872 | tf_op jit(solution)/shard_map/ppermute | solution.py:148
  56.5 9.4 %copy-start.2 = (bf16[4,64,1024]{2,1,0:T(8,128)(2,1)}, bf16[4,64,1024]{2,1,0:T(8,128)(2,1)S(1)}, u32[]{:S(2)}) copy-start(bf16[4,64,1024]{2,1,0:T(8,128)(2,1)S(1)} %collective-permute-done.6) | copy-start | bytes 1572868
  56.5 11.5 %collective-permute-start.8 = (bf16[4,64,1024]{2,1,0:T(8,128)(2,1)S(1)}, bf16[4,64,1024]{2,1,0:T(8,128)(2,1)}, u32[]{:S(2)}, u32[]{:S(2)}) collective-permute-start(bf16[4,64,1024]{2,1,0:T(8,128)(2,1)S(1)} %collective-permute-done.6), channel_id=1, source_target_pairs={{0,1},{1,2},{2,3},{3,4},{4,5},{5,6},{6,7},{7,8},{8,9},{9,10},{10,1... | collective-permute-start | bytes 1572872 | tf_op jit(solution)/shard_map/ppermute | solution.py:145
  65.9 17.7 %collective-permute-start.9 = (bf16[4,64,1024]{2,1,0:T(8,128)(2,1)}, bf16[4,64,1024]{2,1,0:T(8,128)(2,1)S(1)}, u32[]{:S(2)}, u32[]{:S(2)}) collective-permute-start(bf16[4,64,1024]{2,1,0:T(8,128)(2,1)} %collective-permute-done.7), channel_id=1, source_target_pairs={{0,15},{1,0},{2,1},{3,2},{4,3},{5,4},{6,5},{7,6},{8,7},{9,8},{10,9... | collective-permute-start | bytes 1572872 | tf_op jit(solution)/shard_map/ppermute | solution.py:148
  68.0 16.5 %collective-permute-start.10 = (bf16[4,64,1024]{2,1,0:T(8,128)(2,1)}, bf16[4,64,1024]{2,1,0:T(8,128)(2,1)}, u32[]{:S(2)}, u32[]{:S(2)}) collective-permute-start(bf16[4,64,1024]{2,1,0:T(8,128)(2,1)} %collective-permute-done.8), channel_id=1, source_target_pairs={{0,1},{1,2},{2,3},{3,4},{4,5},{5,6},{6,7},{7,8},{8,9},{9,10},{10,1... | collective-permute-start | bytes 1572872 | tf_op jit(solution)/shard_map/ppermute | solution.py:145
  83.6 16.5 %collective-permute-start.11 = (bf16[4,64,1024]{2,1,0:T(8,128)(2,1)S(1)}, bf16[4,64,1024]{2,1,0:T(8,128)(2,1)S(1)}, u32[]{:S(2)}, u32[]{:S(2)}) collective-permute-start(bf16[4,64,1024]{2,1,0:T(8,128)(2,1)S(1)} %collective-permute-done.9), channel_id=1, source_target_pairs={{0,15},{1,0},{2,1},{3,2},{4,3},{5,4},{6,5},{7,6},{8,7},{9,8},{10,9... | collective-permute-start | bytes 1572872 | tf_op jit(solution)/shard_map/ppermute | solution.py:148
  84.5 17.5 %collective-permute-start.12 = (bf16[4,64,1024]{2,1,0:T(8,128)(2,1)}, bf16[4,64,1024]{2,1,0:T(8,128)(2,1)S(1)}, u32[]{:S(2)}, u32[]{:S(2)}) collective-permute-start(bf16[4,64,1024]{2,1,0:T(8,128)(2,1)} %collective-permute-done.10), channel_id=1, source_target_pairs={{0,1},{1,2},{2,3},{3,4},{4,5},{5,6},{6,7},{7,8},{8,9},{9,10},{10,1... | collective-permute-start | bytes 1572872 | tf_op jit(solution)/shard_map/ppermute | solution.py:145
  100.1 13.5 %collective-permute-start.13 = (bf16[4,64,1024]{2,1,0:T(8,128)(2,1)S(1)}, bf16[4,64,1024]{2,1,0:T(8,128)(2,1)S(1)}, u32[]{:S(2)}, u32[]{:S(2)}) collective-permute-start(bf16[4,64,1024]{2,1,0:T(8,128)(2,1)S(1)} %collective-permute-done.11), channel_id=1, source_target_pairs={{0,15},{1,0},{2,1},{3,2},{4,3},{5,4},{6,5},{7,6},{8,7},{9,8},{10,9... | collective-permute-start | bytes 1572872 | tf_op jit(solution)/shard_map/ppermute | solution.py:148
  102.0 12.5 %collective-permute-start.14 = (bf16[4,64,1024]{2,1,0:T(8,128)(2,1)S(1)}, bf16[4,64,1024]{2,1,0:T(8,128)(2,1)S(1)}, u32[]{:S(2)}, u32[]{:S(2)}) collective-permute-start(bf16[4,64,1024]{2,1,0:T(8,128)(2,1)S(1)} %collective-permute-done.12), channel_id=1, source_target_pairs={{0,1},{1,2},{2,3},{3,4},{4,5},{5,6},{6,7},{7,8},{8,9},{9,10},{10,1... | collective-permute-start | bytes 1572872 | tf_op jit(solution)/shard_map/ppermute | solution.py:145
  118.8 4.7 %copy-start.1 = (bf16[128,1024]{1,0:T(8,128)(2,1)S(1)}, bf16[128,1024]{1,0:T(8,128)(2,1)}, u32[]{:S(2)}) copy-start(bf16[128,1024]{1,0:T(8,128)(2,1)} %param.8) | copy-start | bytes 786436
  118.9 5.3 %copy-start.4 = (f32[128,1024]{1,0:T(8,128)S(1)}, f32[128,1024]{1,0:T(8,128)}, u32[]{:S(2)}) copy-start(f32[128,1024]{1,0:T(8,128)} %param.9) | copy-start | bytes 1572868
  123.5 18.5 %copy-start.5 = (f32[512]{0:T(512)S(1)}, f32[512]{0:T(512)}, u32[]{:S(2)}) copy-start(f32[512]{0:T(512)} %param.15) | copy-start | bytes 6148
  124.7 17.9 %copy-start = (f32[128,1024]{1,0:T(8,128)}, f32[128,1024]{1,0:T(8,128)S(1)}, u32[]{:S(2)}) copy-start(f32[128,1024]{1,0:T(8,128)S(1)} %convolution_subtract_fusion) | copy-start | bytes 1572868
  127.4 14.6 %all-to-all-start = ((f32[8,1,512]{2,1,0:T(1,128)}), f32[8,1,512]{2,1,0:T(1,128)S(1)}, u32[]{:S(2)}, u32[]{:S(2)}) async-start(f32[8,1,512]{2,1,0:T(1,128)} %broadcast_in_dim.24), calls=%async_computation | async-start | bytes 32768 | tf_op jit(solution)/shard_map/all_to_all | solution.py:182
